TPU v7x, 512 devices: a whole 4x8x8 slice. The times are simulated.
512 devices in a mesh: front: 8 (over z), grid: 16 (over y, x_hi), depth: 4 (over x_lo, core).
Axes of the slice: x: 4 (x_hi: 2, x_lo: 2; x = x_hi * 2 + x_lo), y: 8, z: 8, core: 2. Of those that a mesh axis runs over, the one named last changes fastest.
Arguments:
- panel_base: float32 [8, 1, 16, 256, 256], P('front', None, 'grid'), as said below
- slab_base: float32 [8, 1, 16, 256, 1024], P('front', None, 'grid', None, 'depth'), may hold values from -6 to 6
- child_tiles: float32 [8, 16, 4, 14, 256, 256], P('front', 'grid', 'depth'), may hold values from -3 to 3
- child_maps: int32 [8, 16, 4, 14, 2], P('front', 'grid', 'depth'), may hold values from 0 to 15, as said below
- front_orders: int32 [8], P('front'), may hold values from 1280 to 4096, as said below
Outputs:
- panel_factor: float32 [8, 1, 16, 256, 256], P('front', None, 'grid')
- schur: float32 [8, 1, 16, 256, 1024], P('front', None, 'grid', None, 'depth')
Inputs may be any that keep to these rules, and one draw needn't show every extreme that they name: Rows r = 0, g = 0 of each front's panel_base form a symmetric positive definite tile. `child_maps`: entry 0 is a parent tile row, entry 1 a tile column from 0 to 4, never both 0. A tile's owner is its parent tile row modulo 16; among one device's 14 tiles at most 2 have the same owner, and in every front one owner receives exactly 2 tiles from every device. `front_orders`: A multiple of 256; in every draw some front has the order 4096.
All inputs are finite; a program needn't handle non-finite values.
Results may differ from a plain program's by a relative error of at most 0.0003.
Values sent between devices are 32-bit elements; how exact they have to be, the bound alone decides.
No kernel may reach another device: no remote copies, remote signals or barrier semaphores. Data moves between devices by JAX's collectives and lax.ppermute only.
A program may use at most 64 MiB of HBM per device.

v0:
```python
import jax
import jax.numpy as jnp
from jax import lax
from jax.sharding import PartitionSpec as P

CAP = 2


def from_root(x, axis, root):
    mine = lax.axis_index(axis) == root
    return lax.psum(jnp.where(mine, x, jnp.zeros_like(x)), axis)


def on_device(panel_base, slab_base, child_tiles, child_maps, front_orders):
    grid_size = lax.axis_size("grid")
    depth_size = lax.axis_size("depth")
    grid_pos = lax.axis_index("grid")
    depth_pos = lax.axis_index("depth")
    fronts_here = panel_base.shape[0]
    rounds = panel_base.shape[1]
    tile_size = panel_base.shape[3]
    column_share = slab_base.shape[4] // tile_size
    next_tiles = column_share * depth_size
    positions = rounds * (next_tiles + 1)
    tile_maps = child_maps[:, 0, 0]
    tile_data = child_tiles[:, 0, 0]
    kid_count = tile_data.shape[1]
    parent_row = tile_maps[..., 0]
    parent_col = tile_maps[..., 1]
    owners = parent_row % grid_size
    same_owner = owners[:, :, None] == owners[:, None, :]
    earlier = jnp.arange(kid_count)[None, :] < jnp.arange(kid_count)[:, None]
    bucket_slot = jnp.sum((same_owner & earlier[None]).astype(jnp.int32), axis=2)
    destination = owners * CAP + bucket_slot
    routing = (destination[:, None, :] == jnp.arange(grid_size * CAP)[None, :, None]).astype(
        jnp.float32
    )
    send_tiles = jnp.einsum("fsk,fkab->fsab", routing, tile_data, precision=lax.Precision.HIGHEST)
    send_tiles = send_tiles.reshape(fronts_here, grid_size, CAP, tile_size, tile_size)
    position = parent_row // grid_size * (next_tiles + 1) + parent_col
    placing = (position[..., None] == jnp.arange(positions)[None, None, :]).astype(jnp.float32)
    send_places = jnp.einsum("fsk,fkp->fsp", routing, placing, precision=lax.Precision.HIGHEST)
    send_places = send_places.reshape(fronts_here, grid_size, CAP, positions)
    arrived, arrived_places = (
        lax.all_to_all(send_tiles, "grid", split_axis=1, concat_axis=1, tiled=True),
        lax.all_to_all(send_places, "grid", split_axis=1, concat_axis=1, tiled=True),
    )
    partial_value = jnp.einsum(
        "fskp,fskab->fpab", arrived_places, arrived, precision=lax.Precision.HIGHEST
    )
    partial_value = partial_value.reshape(fronts_here, rounds, next_tiles + 1, tile_size, tile_size)
    panel_part = partial_value[:, :, 0]
    slab_part = partial_value[:, :, 1:]
    panel_sum, slab_sum = lax.psum((panel_part, slab_part), "depth")
    slab_mine = lax.dynamic_slice_in_dim(slab_sum, depth_pos * column_share, column_share, 2)
    tile_index = jnp.arange(rounds) * grid_size + grid_pos
    live_rows = ((tile_index * tile_size)[None, :] < front_orders[:, None]).astype(jnp.float32)
    front_panel = (panel_base[:, :, 0] + panel_sum) * live_rows[:, :, None, None]
    slab_cols = slab_mine.transpose(0, 1, 3, 2, 4).reshape(
        fronts_here, rounds, tile_size, column_share * tile_size
    )
    front_slab = (slab_base[:, :, 0] + slab_cols) * live_rows[:, :, None, None]
    corner_tile = from_root(front_panel[:, 0], "grid", 0)
    factor = jnp.linalg.cholesky(corner_tile)
    solved = lax.linalg.triangular_solve(
        factor[:, None], front_panel, left_side=False, lower=True, transpose_a=True
    )
    first_tile = (tile_index == 0)[None, :, None, None]
    factored = jnp.where(first_tile, factor[:, None], solved)
    gathered = lax.all_gather(factored[:, :, None], "grid", axis=2, tiled=True)
    flattened = gathered.reshape(fronts_here, rounds * grid_size, tile_size, tile_size)
    wanted = lax.dynamic_slice_in_dim(flattened, 1 + depth_pos * column_share, column_share, 1)
    update = jnp.einsum("frai,fjbi->frajb", factored, wanted, precision=lax.Precision.HIGHEST)
    update = update.reshape(fronts_here, rounds, tile_size, column_share * tile_size)
    schur_block = front_slab - update
    return (factored[:, :, None], schur_block[:, :, None])


def solution(mesh):
    in_specs = (
        P("front", None, "grid", None, None),
        P("front", None, "grid", None, "depth"),
        P("front", "grid", "depth", None, None, None),
        P("front", "grid", "depth", None, None),
        P("front"),
    )
    out_specs = (P("front", None, "grid", None, None), P("front", None, "grid", None, "depth"))
    return jax.shard_map(
        on_device, mesh=mesh, in_specs=in_specs, out_specs=out_specs, check_vma=False
    )
```

profile of v0, /device:TPU:8, one launch (start us, length us, event | category | flops | bytes accessed | tf_op | source)
XLA Modules:
  0.0 655.4 jit_solution(3843907014376865639)
XLA Ops:
  7.2 0.7 and_select_fusion.2
  7.9 0.8 add_bitcast_fusion
  9.0 0.7 multiply_add_fusion.1
  9.9 0.7 copy.40
  10.7 10.0 %all-to-all-start = ((f32[1,16,2,5]{3,2,0,1:T(2,128)}), f32[1,16,2,5]{3,2,0,1:T(2,128)S(1)}, u32[]{:S(2)}, u32[]{:S(2)}) async-start(f32[1,16,2,5]{3,2,0,1:T(2,128)} %copy.40), calls=%async_computation | async-start | bytes 32768 | tf_op jit(solution)/shard_map/all_to_all | solution.py:46
  20.7 7.5 %fusion.6 = f32[1,16,2,256,256]{4,1,3,2,0:T(8,128)S(1)} fusion(f32[14,256,256]{2,1,0:T(8,128)} %bitcast.124, s32[16,2]{0,1:T(2,128)S(1)} %multiply_add_fusion, s32[14]{0:T(128)S(1)} %multiply_add_fusion.1), kind=kOutput, calls=%fused_computation.9 | convolution fusion | flops 352321984 | bytes 12058808 | tf_op jit(solution)/shard_map/fsk,fkab->fsab/dot_general | solution.py:38
  28.2 8.1 %copy.43 = f32[1,16,2,256,256]{4,3,2,0,1:T(8,128)} copy(f32[1,16,2,256,256]{4,1,3,2,0:T(8,128)S(1)} %fusion.6) | data formatting | bytes 16777216 | tf_op jit(solution)/shard_map/fsk,fkab->fsab/dot_general | solution.py:38
  36.2 9.6 %all-to-all-start.1 = ((f32[1,16,2,256,256]{4,3,2,0,1:T(8,128)}), f32[1,16,2,256,256]{4,3,2,0,1:T(8,128)}, u32[]{:S(2)}, u32[]{:S(2)}) async-start(f32[1,16,2,256,256]{4,3,2,0,1:T(8,128)} %copy.43), calls=%async_computation.1 | async-start | bytes 16777216 | tf_op jit(solution)/shard_map/all_to_all | solution.py:45
  46.2 191.3 %all-to-all-done.1 = f32[1,16,2,256,256]{4,3,2,0,1:T(8,128)} async-done(((f32[1,16,2,256,256]{4,3,2,0,1:T(8,128)}), f32[1,16,2,256,256]{4,3,2,0,1:T(8,128)}, u32[]{:S(2)}, u32[]{:S(2)}) %all-to-all-start.1) | async-done | bytes 8388640 | tf_op jit(solution)/shard_map/all_to_all | solution.py:45
  237.4 12.4 %fusion.9 = f32[5,256,256]{2,0,1:T(8,128)S(1)} fusion(f32[1,16,2,256,256]{4,3,2,0,1:T(8,128)} %all-to-all-done.1, f32[1,16,2,5]{1,3,2,0:T(8,128)S(1)} %copy.41), kind=kOutput, calls=%fused_computation.10 | convolution fusion | flops 125829120 | bytes 9699968 | tf_op jit(solution)/shard_map/fskp,fskab->fpab/dot_general | solution.py:48
  249.9 0.7 copy.45
  250.5 0.7 slice_bitcast_fusion
  251.3 1.0 slice.74
  253.0 1.1 copy.39
  254.1 56.0 %all-reduce.7.cloned.1.call-done = (f32[1,1,256,256]{2,3,1,0:T(8,128)}, f32[1,1,4,256,256]{3,4,2,1,0:T(8,128)}) async-done(((f32[1,1,256,256]{2,3,1,0:T(8,128)}, f32[1,1,4,256,256]{3,4,2,1,0:T(8,128)}), (f32[1,1,256,256]{2,3,1,0:T(8,128)}, f32[1,1,4,256,256]{3,4,2,1,0:T(8,128)})) %all-reduce.7.cloned.1.call-update) | async-done | bytes 1310736 | tf_op jit(solution)/shard_map/psum | solution.py:54
  310.2 1.7 select_bitcast_fusion
  312.0 166.2 %all-reduce.5.cloned.1.call-done = f32[1,256,256]{1,2,0:T(8,128)} async-done(((f32[1,256,256]{1,2,0:T(8,128)}), f32[1,256,256]{1,2,0:T(8,128)}) %all-reduce.5.cloned.1.call-update) | async-done | bytes 262160 | tf_op jit(solution)/shard_map/psum | solution.py:11
  478.2 1.1 copy.46
  479.3 1.0 fusion.21
  480.3 11.7 %custom-call.16 = f32[1,128,128]{2,1,0:T(8,128)S(1)} custom-call(f32[1,128,128]{2,1,0:T(8,128)S(1)} %cholesky.114), custom_call_target="Cholesky" | custom-call | tf_op jit(solution)/shard_map/jit(cholesky)/cholesky | solution.py:64
  492.1 9.8 %custom-call.17 = f32[1,1,128,128]{2,3,1,0:T(8,128)S(1)} custom-call(f32[1,1,128,128]{3,2,1,0:T(8,128)S(1)} %get-tuple-element.45), custom_call_target="InvertDiagBlocksLowerTriangular" | custom-call | tf_op jit(solution)/shard_map/jit(cholesky)/cholesky | solution.py:64
  502.5 11.7 %custom-call.18 = f32[1,128,128]{2,1,0:T(8,128)S(1)} custom-call(f32[1,128,128]{2,1,0:T(8,128)S(1)} %fusion.15), custom_call_target="Cholesky" | custom-call | tf_op jit(solution)/shard_map/jit(cholesky)/cholesky | solution.py:64
  514.4 0.7 compare_reduce_fusion
  516.5 4.4 while.1
  517.3 1.4 constant_dynamic-slice_fusion.5
  519.4 1.4 constant_dynamic-slice_fusion.5
  520.9 19.7 %custom-call.19 = f32[1,1,2,128,128]{3,4,2,1,0:T(8,128)S(1)} custom-call(f32[1,1,2,128,128]{4,3,2,1,0:T(8,128)S(1)} %bitcast.132), custom_call_target="InvertDiagBlocksLowerTriangular" | custom-call | tf_op jit(solution)/shard_map/triangular_solve | solution.py:65
  541.6 0.8 copy.53
  542.6 0.8 copy.55
  543.4 103.2 %all-gather.2.cloned.1.call-done = f32[1,1,16,256,256]{4,3,1,0,2:T(8,128)} async-done(((f32[1,1,1,256,256]{4,3,1,0,2:T(8,128)}), f32[1,1,16,256,256]{4,3,1,0,2:T(8,128)}) %all-gather.2.cloned.1.call-update) | async-done | bytes 4194320 | tf_op jit(solution)/shard_map/all_gather | solution.py:70
  646.6 1.5 fusion.12
  648.0 0.8 copy.56
  (42 shorter events, 4.5 us)
Async XLA Ops:
  10.7 25.6 %all-to-all-start = ((f32[1,16,2,5]{3,2,0,1:T(2,128)}), f32[1,16,2,5]{3,2,0,1:T(2,128)S(1)}, u32[]{:S(2)}, u32[]{:S(2)}) async-start(f32[1,16,2,5]{3,2,0,1:T(2,128)} %copy.40), calls=%async_computation | async-start | bytes 32768 | tf_op jit(solution)/shard_map/all_to_all | solution.py:46
  36.2 201.2 %all-to-all-start.1 = ((f32[1,16,2,256,256]{4,3,2,0,1:T(8,128)}), f32[1,16,2,256,256]{4,3,2,0,1:T(8,128)}, u32[]{:S(2)}, u32[]{:S(2)}) async-start(f32[1,16,2,256,256]{4,3,2,0,1:T(8,128)} %copy.43), calls=%async_computation.1 | async-start | bytes 16777216 | tf_op jit(solution)/shard_map/all_to_all | solution.py:45
  45.9 264.3 %all-reduce.7.cloned.1.call-start = ((), (), s32[]{:S(2)}) async-start(), calls=%async_computation.4 | async-start | bytes 2621440 | tf_op jit(solution)/shard_map/psum | solution.py:54
  252.3 225.9 %all-reduce.5.cloned.1.call-start = ((), (), s32[]{:S(2)}) async-start(), calls=%async_computation.2 | async-start | bytes 524288 | tf_op jit(solution)/shard_map/psum | solution.py:11
  311.9 334.7 %all-gather.2.cloned.1.call-start = ((), (), s32[]{:S(2)}) async-start(), calls=%async_computation.3 | async-start | bytes 4456448 | tf_op jit(solution)/shard_map/all_gather | solution.py:70
  312.0 230.5 %copy-start = (f32[1,1,1,256,256]{4,3,2,1,0:T(8,128)S(1)}, f32[1,1,1,256,256]{4,3,2,1,0:T(8,128)}, u32[]{:S(2)}) copy-start(f32[1,1,1,256,256]{4,3,2,1,0:T(8,128)} %param.6) | copy-start | bytes 786436
Sparse Core Ops, SparseCore 0:
  252.5 57.6 all-reduce.6
  313.6 164.4 all-reduce.4
  542.6 103.9 all-gather.1
where the time goes:
time: 656 us; the launch traced here: 655 us
  waiting for transfers between devices  517 us (79%)
  other arithmetic  59 us (9%)
  matrix products  23 us (4%)
  local copies, waits for them, and re-layouts  20.6 us (3%)
  starting transfers between devices  20 us (3%)
  between operations  15.9 us (2%)
    all_to_all x1, waiting for transfers between devices, on_device(): lax.all_to_all(send_tiles, 'grid', split_axis=1, concat_axis=1, tiled=True)  191 us
    psum x1, waiting for transfers between devices, from_root(): return lax.psum(jnp.where(mine, x, jnp.zeros_like(x)), axis)  166 us
    all_gather x1, waiting for transfers between devices, on_device(): gathered = lax.all_gather(factored[:, :, None], 'grid', axis=2, tiled=True)  103 us
    psum x1, waiting for transfers between devices, on_device(): panel_sum, slab_sum = lax.psum((panel_part, slab_part), 'depth')  56 us
    another operation x6, other arithmetic, on_device(): factor = jnp.linalg.cholesky(corner_tile)  34 us
    another operation x3, other arithmetic, on_device(): lax.linalg.triangular_solve(factor[:, None], front_panel, left_side=False...  19.7 us
  transfers between devices with their start and end apart: 5, of which 4 were waited for; matrix products, arithmetic and copies ran while one was open for 3% of the time, Pallas kernels for 0%

commit v1 on v0

v1 whole, which is shorter than its diff:
```python
import jax
import jax.numpy as jnp
from jax import lax
from jax.experimental import pallas as pl
from jax.experimental.pallas import tpu as pltpu
from jax.sharding import PartitionSpec as P

CAP = 2
HIGH = lax.Precision.HIGHEST


def accumulate(place, arrived, positions):
    slots, tile, _ = arrived.shape

    def kernel(place_ref, x_ref, o_ref):
        o_ref[...] = jnp.zeros_like(o_ref)

        def body(s, carry):
            p = place_ref[s]
            o_ref[p] = o_ref[p] + x_ref[s]
            return carry

        lax.fori_loop(0, slots, body, 0)

    return pl.pallas_call(
        kernel,
        grid_spec=pltpu.PrefetchScalarGridSpec(
            num_scalar_prefetch=1,
            grid=(1,),
            in_specs=[pl.BlockSpec((slots, tile, tile), lambda i, p: (0, 0, 0))],
            out_specs=pl.BlockSpec((positions + 1, tile, tile), lambda i, p: (0, 0, 0)),
        ),
        out_shape=jax.ShapeDtypeStruct((positions + 1, tile, tile), jnp.float32),
    )(place, arrived)


def route(src, tiles, slots):
    kids, tile, _ = tiles.shape

    def kernel(src_ref, x_ref, o_ref):
        def body(s, carry):
            k = src_ref[s]
            valid = k < kids
            kk = jnp.minimum(k, kids - 1)
            o_ref[s] = jnp.where(valid, x_ref[kk], 0.0)
            return carry

        lax.fori_loop(0, slots, body, 0)

    return pl.pallas_call(
        kernel,
        grid_spec=pltpu.PrefetchScalarGridSpec(
            num_scalar_prefetch=1,
            grid=(1,),
            in_specs=[pl.BlockSpec((kids, tile, tile), lambda i, s: (0, 0, 0))],
            out_specs=pl.BlockSpec((slots, tile, tile), lambda i, s: (0, 0, 0)),
        ),
        out_shape=jax.ShapeDtypeStruct((slots, tile, tile), jnp.float32),
    )(src, tiles)


def on_device(panel_base, slab_base, child_tiles, child_maps, front_orders):
    grid_size = lax.axis_size("grid")
    depth_size = lax.axis_size("depth")
    grid_pos = lax.axis_index("grid")
    depth_pos = lax.axis_index("depth")
    rounds = panel_base.shape[1]
    tile = panel_base.shape[3]
    column_share = slab_base.shape[4] // tile
    next_tiles = column_share * depth_size
    positions = rounds * (next_tiles + 1)
    assert rounds == 1 and column_share == 1 and depth_size == 4
    assert panel_base.shape[0] == 1

    corner = panel_base[0, 0, 0]
    have = grid_pos == 0
    steps = []
    s = 1
    while s < grid_size:
        steps.append(s)
        s *= 2
    for s in reversed(steps):
        perm = [(i, i + s) for i in range(grid_size) if i % (2 * s) == 0 and i + s < grid_size]
        got = lax.ppermute(corner, "grid", perm)
        is_dst = (grid_pos % (2 * s)) == s
        corner = jnp.where(is_dst, got, corner)
    factor = jnp.linalg.cholesky(corner)
    eye = jnp.eye(tile, dtype=jnp.float32)
    inv_t = lax.linalg.triangular_solve(factor, eye, left_side=True, lower=True, transpose_a=True)

    tile_maps = child_maps[0, 0, 0]
    tile_data = child_tiles[0, 0, 0]
    kid_count = tile_data.shape[0]
    parent_row = tile_maps[:, 0]
    parent_col = tile_maps[:, 1]
    owners = parent_row % grid_size
    same_owner = owners[:, None] == owners[None, :]
    earlier = jnp.arange(kid_count)[None, :] < jnp.arange(kid_count)[:, None]
    bucket_slot = jnp.sum((same_owner & earlier).astype(jnp.int32), axis=1)
    destination = owners * CAP + bucket_slot
    slots = grid_size * CAP
    hit = destination[None, :] == jnp.arange(slots)[:, None]
    kid_ids = jnp.arange(kid_count, dtype=jnp.int32)
    src = jnp.sum(jnp.where(hit, kid_ids[None, :], 0), axis=1) + jnp.where(
        jnp.any(hit, axis=1), 0, kid_count
    )
    src = src.astype(jnp.int32)
    position = (parent_row // grid_size * (next_tiles + 1) + parent_col).astype(jnp.int32)
    send_place = jnp.sum(jnp.where(hit, position[None, :], 0), axis=1) + jnp.where(
        jnp.any(hit, axis=1), 0, positions
    )
    send_place = send_place.astype(jnp.int32)
    send_tiles = route(src, tile_data, slots).reshape(grid_size, CAP, tile, tile)
    arrived = lax.all_to_all(send_tiles, "grid", 0, 0, tiled=True)
    arrived_place = lax.all_to_all(send_place.reshape(grid_size, CAP), "grid", 0, 0, tiled=True)
    partial = accumulate(arrived_place.reshape(slots), arrived.reshape(slots, tile, tile), positions)

    panel_part = partial[0]
    slab_part = partial[1:positions]
    core_bit = depth_pos % 2
    chip_bit = depth_pos // 2
    other = 1 - core_bit
    send1 = jnp.stack([panel_part, slab_part[other], slab_part[other + 2]])
    keep1 = jnp.stack([panel_part, slab_part[core_bit], slab_part[core_bit + 2]])
    got1 = lax.ppermute(send1, "depth", [(0, 1), (1, 0), (2, 3), (3, 2)])
    sum1 = keep1 + got1
    send2 = jnp.stack([sum1[0], sum1[1 + (1 - chip_bit)]])
    got2 = lax.ppermute(send2, "depth", [(0, 2), (2, 0), (1, 3), (3, 1)])
    panel_sum = sum1[0] + got2[0]
    slab_sum = sum1[1 + chip_bit] + got2[1]

    live = (grid_pos * tile < front_orders[0]).astype(jnp.float32)
    front_panel = (panel_base[0, 0, 0] + panel_sum) * live
    front_slab = (slab_base[0, 0, 0] + slab_sum) * live

    solved = jnp.dot(front_panel, inv_t, precision=HIGH)
    factored = jnp.where(grid_pos == 0, factor, solved)

    wanted = factored
    for s in reversed(steps):
        perm = []
        for d in range(depth_size):
            for v in range(0, grid_size, 2 * s):
                if v + s < grid_size:
                    g_src = (v + d + 1) % grid_size
                    g_dst = (v + s + d + 1) % grid_size
                    perm.append((g_src * depth_size + d, g_dst * depth_size + d))
        got = lax.ppermute(wanted, ("grid", "depth"), perm)
        v_here = (grid_pos - depth_pos - 1) % grid_size
        is_dst = (v_here % (2 * s)) == s
        wanted = jnp.where(is_dst, got, wanted)

    update = lax.dot_general(
        factored, wanted, (((1,), (1,)), ((), ())), precision=HIGH
    )
    schur_block = front_slab - update
    return (factored[None, None, None], schur_block[None, None, None])


def solution(mesh):
    in_specs = (
        P("front", None, "grid", None, None),
        P("front", None, "grid", None, "depth"),
        P("front", "grid", "depth", None, None, None),
        P("front", "grid", "depth", None, None),
        P("front"),
    )
    out_specs = (P("front", None, "grid", None, None), P("front", None, "grid", None, "depth"))
    return jax.shard_map(
        on_device, mesh=mesh, in_specs=in_specs, out_specs=out_specs, check_vma=False
    )
```

time: 656 us -> 372 us (0.57)
  the two profiles are of different devices: /device:TPU:8 before, /device:TPU:330 now
where the time goes in v1:
time: 372 us
  waiting for transfers between devices  252 us (68%)
  other arithmetic  58.6 us (16%)
  starting transfers between devices  30.2 us (8%)
  Pallas kernels  13.5 us (4%)
  local copies, waits for them, and re-layouts  9.69 us (3%)
  matrix products  4.44 us (1%)
    ppermute x4, waiting for transfers between devices, on_device(): got = lax.ppermute(corner, 'grid', perm)  204 us
    ppermute x4, waiting for transfers between devices, on_device(): got = lax.ppermute(wanted, ('grid', 'depth'), perm)  36.5 us
    another operation x6, other arithmetic, on_device(): factor = jnp.linalg.cholesky(corner)  34 us
    another operation x3, other arithmetic, on_device(): lax.linalg.triangular_solve(factor, eye, left_side=True, lower=True, tran...  21.1 us
    ppermute x1, waiting for transfers between devices, on_device(): got2 = lax.ppermute(send2, 'depth', [(0, 2), (2, 0), (1, 3), (3, 1)])  10.4 us
    all_to_all x1, starting transfers between devices, on_device(): lax.all_to_all(send_place.reshape(grid_size, CAP), 'grid', 0, 0, tiled=True)  9.12 us
    all_to_all x1, starting transfers between devices, on_device(): arrived = lax.all_to_all(send_tiles, 'grid', 0, 0, tiled=True)  8.34 us
  transfers between devices with their start and end apart: 12, of which 5 were waited for; matrix products, arithmetic and copies ran while one was open for 18% of the time, Pallas kernels for 2%

profile of v1, /device:TPU:330, one launch (start us, length us, event | category | flops | bytes accessed | tf_op | source)
XLA Modules:
  0.0 371.6 jit_solution(5698927189814480362)
XLA Ops:
  0.6 0.8 bitcast_add_fusion.1
  1.4 0.7 fusion.32
  3.0 0.7 add.180
  3.7 9.1 %all-to-all-start = ((s32[16,1,2]{2,1,0:T(1,128)}), s32[16,1,2]{2,1,0:T(1,128)S(1)}, u32[]{:S(2)}, u32[]{:S(2)}) async-start(s32[16,1,2]{2,1,0:T(1,128)} %bitcast.8), calls=%async_computation | async-start | bytes 16384 | tf_op jit(solution)/shard_map/all_to_all | solution.py:115
  12.8 7.2 %shard_map.68 = f32[32,256,256]{2,1,0:T(8,128)} custom-call(s32[32]{0:T(128)} %get-tuple-element.34.src_ref, f32[14,256,256]{2,1,0:T(8,128)} %bitcast.86), custom_call_target="tpu_custom_call" | custom-call | tf_op jit(solution)/shard_map/pallas_call | solution.py:50
  20.0 1.4 all-to-all-done
  21.4 8.3 %all-to-all-start.1 = ((f32[16,2,256,256]{3,2,1,0:T(8,128)}), f32[16,2,256,256]{3,2,1,0:T(8,128)}, u32[]{:S(2)}, u32[]{:S(2)}) async-start(f32[16,2,256,256]{3,2,1,0:T(8,128)} %bitcast.85), calls=%async_computation.1 | async-start | bytes 16777216 | tf_op jit(solution)/shard_map/all_to_all | solution.py:114
  29.7 0.7 collective-permute-start
  30.5 0.7 collective-permute-start.1
  31.3 1.3 collective-permute-start.2
  32.6 202.4 %collective-permute-done.2 = f32[256,256]{1,0:T(8,128)S(1)} collective-permute-done((f32[256,256]{1,0:T(8,128)S(1)}, f32[256,256]{1,0:T(8,128)S(1)}, u32[]{:S(2)}, u32[]{:S(2)}) %collective-permute-start.2) | collective-permute-done | bytes 262176 | tf_op jit(solution)/shard_map/ppermute | solution.py:84
  235.0 1.3 collective-permute-start.3
  238.8 1.3 collective-permute-done.3
  240.4 11.7 %cholesky.50 = f32[128,128]{1,0:T(8,128)S(1)} custom-call(f32[128,128]{1,0:T(8,128)S(1)} %cholesky.118), custom_call_target="Cholesky" | custom-call | tf_op jit(solution)/shard_map/jit(cholesky)/cholesky | solution.py:87
  252.1 9.8 %custom-call.14 = f32[1,128,128]{1,2,0:T(8,128)S(1)} custom-call(f32[1,128,128]{2,1,0:T(8,128)S(1)} %get-tuple-element.33), custom_call_target="InvertDiagBlocksLowerTriangular" | custom-call | tf_op jit(solution)/shard_map/jit(cholesky)/cholesky | solution.py:87
  262.4 11.7 %cholesky.105 = f32[128,128]{1,0:T(8,128)S(1)} custom-call(f32[128,128]{1,0:T(8,128)S(1)} %slice_subtract_fusion), custom_call_target="Cholesky" | custom-call | tf_op jit(solution)/shard_map/jit(cholesky)/cholesky | solution.py:87
  276.1 6.3 %shard_map.69 = f32[6,256,256]{2,1,0:T(8,128)} custom-call(s32[32]{0:T(128)} %reshape.128.place_ref, f32[32,256,256]{2,1,0:T(8,128)} %bitcast.11.x_ref), custom_call_target="tpu_custom_call" | custom-call | tf_op jit(solution)/shard_map/pallas_call | solution.py:25
  282.5 1.0 slice.83
  283.4 1.3 slice.84
  285.0 2.1 collective-permute-start.4
  287.2 5.2 %while.1 = (s32[]{:T(128)}, f32[256,256]{1,0:T(8,128)S(1)}, s32[2,2]{1,0:T(2,128)S(1)}, f32[2,128,128]{2,1,0:T(8,128)}, s32[]{:T(128)}) while((s32[]{:T(128)}, f32[256,256]{1,0:T(8,128)S(1)}, s32[2,2]{1,0:T(2,128)S(1)}, f32[2,128,128]{2,1,0:T(8,128)}, s32[]{:T(128)}) %tuple.34), condition=%wide.while_cond, body=%wide.while_body.sunk | while | flops 2 | bytes 132205 | solution.py:89
  287.8 2.0 bitcast_dynamic-update-slice_fusion.2
  290.4 2.0 bitcast_dynamic-update-slice_fusion.2
  292.4 21.1 %custom-call.15 = f32[2,128,128]{1,2,0:T(8,128)} custom-call(f32[2,128,128]{2,1,0:T(8,128)} %get-tuple-element.9), custom_call_target="InvertDiagBlocksLowerTriangular" | custom-call | tf_op jit(solution)/shard_map/triangular_solve | solution.py:89
  313.7 3.3 collective-permute-start.5
  317.0 1.0 fusion.22
  318.4 1.1 fusion.26
  319.5 10.4 %collective-permute-done.5 = f32[2,256,256]{2,1,0:T(8,128)S(1)} collective-permute-done((f32[2,256,256]{2,1,0:T(8,128)S(1)}, f32[2,256,256]{2,1,0:T(8,128)S(1)}, u32[]{:S(2)}, u32[]{:S(2)}) %collective-permute-start.5) | collective-permute-done | bytes 524320 | tf_op jit(solution)/shard_map/ppermute | solution.py:128
  330.3 0.7 collective-permute-start.6
  332.6 1.3 collective-permute-start.9
  333.9 36.5 %collective-permute-done.9 = f32[256,256]{1,0:T(8,128)S(1)} collective-permute-done((f32[256,256]{1,0:T(8,128)S(1)}, f32[256,256]{1,0:T(8,128)S(1)}, u32[]{:S(2)}, u32[]{:S(2)}) %collective-permute-start.9) | collective-permute-done | bytes 262176 | tf_op jit(solution)/shard_map/ppermute | solution.py:148
  370.5 1.1 fusion.7
  (56 shorter events, 8.1 us)
Async XLA Ops:
  3.7 17.7 %all-to-all-start = ((s32[16,1,2]{2,1,0:T(1,128)}), s32[16,1,2]{2,1,0:T(1,128)S(1)}, u32[]{:S(2)}, u32[]{:S(2)}) async-start(s32[16,1,2]{2,1,0:T(1,128)} %bitcast.8), calls=%async_computation | async-start | bytes 16384 | tf_op jit(solution)/shard_map/all_to_all | solution.py:115
  21.4 8.3 %copy-start.1 = (f32[1,1,1,256,256]{4,3,2,1,0:T(8,128)S(1)}, f32[1,1,1,256,256]{4,3,2,1,0:T(8,128)}, u32[]{:S(2)}) copy-start(f32[1,1,1,256,256]{4,3,2,1,0:T(8,128)} %param.5) | copy-start | bytes 786436
  21.4 254.7 %all-to-all-start.1 = ((f32[16,2,256,256]{3,2,1,0:T(8,128)}), f32[16,2,256,256]{3,2,1,0:T(8,128)}, u32[]{:S(2)}, u32[]{:S(2)}) async-start(f32[16,2,256,256]{3,2,1,0:T(8,128)} %bitcast.85), calls=%async_computation.1 | async-start | bytes 16777216 | tf_op jit(solution)/shard_map/all_to_all | solution.py:114
  29.7 0.7 collective-permute-start
  30.5 0.7 collective-permute-start.1
  31.3 203.7 %collective-permute-start.2 = (f32[256,256]{1,0:T(8,128)S(1)}, f32[256,256]{1,0:T(8,128)S(1)}, u32[]{:S(2)}, u32[]{:S(2)}) collective-permute-start(f32[256,256]{1,0:T(8,128)S(1)} %broadcast_select_fusion.4), channel_id=1, source_target_pairs={{0,8},{16,24},{32,40},{48,56},{1,9},{17,25},{33,41},{49,57},{2,10}... | collective-permute-start | bytes 786440 | tf_op jit(solution)/shard_map/ppermute | solution.py:84
  235.0 5.2 %collective-permute-start.3 = (f32[256,256]{1,0:T(8,128)S(1)}, f32[256,256]{1,0:T(8,128)S(1)}, u32[]{:S(2)}, u32[]{:S(2)}) collective-permute-start(f32[256,256]{1,0:T(8,128)S(1)} %broadcast_select_fusion.5), channel_id=1, source_target_pairs={{0,4},{8,12},{16,20},{24,28},{32,36},{40,44},{48,52},{56,60},{1,5}... | collective-permute-start | bytes 786440 | tf_op jit(solution)/shard_map/ppermute | solution.py:84
  283.4 87.1 %copy-start.2 = (f32[1,1,1,256,256]{4,3,2,1,0:T(8,128)S(1)}, f32[1,1,1,256,256]{4,3,2,1,0:T(8,128)}, u32[]{:S(2)}) copy-start(f32[1,1,1,256,256]{4,3,2,1,0:T(8,128)} %param.6) | copy-start | bytes 786436
  285.0 28.5 %collective-permute-start.4 = (f32[3,256,256]{2,1,0:T(8,128)S(1)}, f32[3,256,256]{2,1,0:T(8,128)S(1)}, u32[]{:S(2)}, u32[]{:S(2)}) collective-permute-start(f32[3,256,256]{2,1,0:T(8,128)S(1)} %fusion.2), channel_id=1, source_target_pairs={{0,1},{1,0},{2,3},{3,2},{4,5},{5,4},{6,7},{7,6},{8,9},{9,8},{10,11... | collective-permute-start | bytes 2359304 | tf_op jit(solution)/shard_map/ppermute | solution.py:125
  313.7 16.2 %collective-permute-start.5 = (f32[2,256,256]{2,1,0:T(8,128)S(1)}, f32[2,256,256]{2,1,0:T(8,128)S(1)}, u32[]{:S(2)}, u32[]{:S(2)}) collective-permute-start(f32[2,256,256]{2,1,0:T(8,128)S(1)} %pad_maximum_fusion.2), channel_id=1, source_target_pairs={{0,2},{2,0},{1,3},{3,1},{4,6},{6,4},{5,7},{7,5},{8,10},{10,8},{9,1... | collective-permute-start | bytes 1572872 | tf_op jit(solution)/shard_map/ppermute | solution.py:128
  330.3 41.3 %copy-start = (f32[256,256]{1,0:T(8,128)}, f32[256,256]{1,0:T(8,128)S(1)}, u32[]{:S(2)}) copy-start(f32[256,256]{1,0:T(8,128)S(1)} %convolution_select_fusion) | copy-start | bytes 786436
  330.3 0.7 collective-permute-start.6
  331.1 0.7 collective-permute-start.7
  331.9 0.7 collective-permute-start.8
  332.6 37.9 %collective-permute-start.9 = (f32[256,256]{1,0:T(8,128)S(1)}, f32[256,256]{1,0:T(8,128)S(1)}, u32[]{:S(2)}, u32[]{:S(2)}) collective-permute-start(f32[256,256]{1,0:T(8,128)S(1)} %broadcast_select_fusion.2), channel_id=1, source_target_pairs={{4,8},{12,16},{20,24},{28,32},{36,40},{44,48},{52,56},{60,0},{9,13... | collective-permute-start | bytes 786440 | tf_op jit(solution)/shard_map/ppermute | solution.py:148
